TPU v7x, 32 devices: a whole 2x2x4 slice. The times are simulated.
32 devices in a mesh: section: 2 (over x), seq: 8 (over z, y), head: 2 (over core).
Axes of the slice: x: 2, y: 2, z: 4, core: 2. Of those that a mesh axis runs over, the one named last changes fastest.
Arguments:
- bwd_input: bfloat16 [2, 1024, 3584], P('section', 'seq', 'head'), may hold values from -6 to 6
- bwd_docs: int32 [2, 1024], P('section', 'seq'), may hold values from 0 to 3, as said below
- bwd_grad: bfloat16 [2, 1024, 3584], P('section', 'seq', 'head'), may hold values from -6 to 6
- proj_weight: bfloat16 [2, 256, 3584], P('section', 'seq', 'head'), may hold values from -0.09375 to 0.09375
- step_weight: float32 [2, 3584], P('section', 'head'), may hold values from -0.75 to 0.75
- step_bias: float32 [2, 56], P('section', 'head'), may hold values from -5 to -2
- rate_log: float32 [2, 56], P('section', 'head'), may hold values from -4 to 0.5
- skip_gain: float32 [2, 56], P('section', 'head'), may hold values from 0.5 to 1.5
Outputs:
- prev_grad: bfloat16 [2, 1024, 3584], P('section', 'seq', 'head')
- grad_proj: float32 [2, 256, 3584], P('section', 'seq', 'head')
- grad_step_weight: float32 [2, 3584], P('section', 'head')
- grad_step_bias: float32 [2, 56], P('section', 'head')
- grad_rate_log: float32 [2, 56], P('section', 'head')
- grad_skip: float32 [2, 56], P('section', 'head')
Inputs may be any that keep to these rules, and one draw needn't show every extreme that they name: `bwd_docs`: document ids of each row never fall, start at 0, every id occurs, and one document of each row holds 512 tokens.
All inputs are finite; a program needn't handle non-finite values.
Results may differ from a plain program's by a relative error of at most 0.023.
Values may be sent and summed in bfloat16 or wider, within the bound.
No kernel may reach another device: no remote copies, remote signals or barrier semaphores. Data moves between devices by JAX's collectives and lax.ppermute only.
A program may use at most 64 MiB of HBM per device.

v0:
```python
import jax
import jax.numpy as jnp
from jax import lax
from jax.sharding import PartitionSpec as P

EXACT = lax.Precision.HIGHEST


def shifted(block, axis, distance):
    devices = range(lax.axis_size(axis))
    route = [(i - distance, i) for i in devices if i - distance in devices]
    return lax.ppermute(block, axis, route)


def contract(spec, left, right):
    return jnp.einsum(spec, left, right, preferred_element_type=jnp.float32)


def local_setup(values, step_weight, step_bias, rate_log):
    tokens = values.shape[0]
    raw_step = (
        jnp.einsum("thp,hp->th", values.astype(jnp.float32), step_weight, precision=EXACT)
        + step_bias[None, :]
    )
    step_size = jax.nn.softplus(raw_step)
    decay_log = -jnp.exp(rate_log)[None, :] * step_size
    row_ids = lax.broadcasted_iota(jnp.int32, (tokens, tokens), 0)
    col_ids = lax.broadcasted_iota(jnp.int32, (tokens, tokens), 1)
    triangle = (row_ids >= col_ids).astype(jnp.float32)
    cumulative = jnp.dot(triangle, decay_log, precision=EXACT)
    return (step_size, cumulative, row_ids, col_ids)


def span_summary(values, mixer, step_weight, step_bias, rate_log, docs, doc_before):
    step_size, cumulative, row_ids, col_ids = local_setup(values, step_weight, step_bias, rate_log)
    final_log = cumulative[-1]
    tail_mask = (docs == docs[-1]).astype(jnp.float32)[:, None]
    tail_weight = (
        jnp.exp(jnp.where(tail_mask > 0, final_log[None, :] - cumulative, 0.0))
        * tail_mask
        * step_size
    )
    unbroken = (docs[-1] == doc_before).astype(jnp.float32)
    carry_decay = jnp.exp(final_log) * unbroken
    half_width = mixer.shape[1] // 2
    writers = mixer[:, :half_width]
    weighted = (tail_weight[:, :, None] * writers.astype(jnp.float32)[:, None, :]).astype(
        jnp.bfloat16
    )
    span_state = contract("thn,thp->hnp", weighted, values)
    return (carry_decay, span_state)


def span_output(
    values, mixer, step_weight, step_bias, rate_log, skip_gain, docs, doc_before, incoming
):
    step_size, cumulative, row_ids, col_ids = local_setup(values, step_weight, step_bias, rate_log)
    half_width = mixer.shape[1] // 2
    writers = mixer[:, :half_width]
    readers = mixer[:, half_width:]
    affinity = jnp.dot(readers, writers.T, preferred_element_type=jnp.float32)
    same_doc = ((docs[:, None] == docs[None, :]) & (row_ids >= col_ids)).astype(jnp.float32)
    heads_first = cumulative.T
    log_gap = heads_first[:, :, None] - heads_first[:, None, :]
    mixing = (
        jnp.exp(jnp.where(same_doc[None] > 0, log_gap, 0.0))
        * same_doc[None]
        * affinity[None]
        * step_size.T[:, None, :]
    )
    mixing = mixing.astype(jnp.bfloat16)
    local_part = contract("hts,shp->thp", mixing, values)
    unbroken = (docs == doc_before).astype(jnp.float32)
    carry_scale = jnp.exp(cumulative) * unbroken[:, None]
    carried = jnp.einsum("tn,hnp->thp", readers.astype(jnp.float32), incoming, precision=EXACT)
    combined = (
        values.astype(jnp.float32) * (1.0 + skip_gain)[None, :, None]
        + local_part
        + carry_scale[:, :, None] * carried
    )
    return combined.astype(jnp.bfloat16)


def scan_rounds(decay, state, axis, forward):
    size, mine = (lax.axis_size(axis), lax.axis_index(axis))
    far_decay, far_state = (decay, state)
    near_decay = jnp.ones_like(decay)
    near_state = jnp.zeros_like(state)
    distance = 1
    while distance < size:
        got_decay, got_state = shifted(
            (far_decay, far_state.astype(jnp.bfloat16)), axis, distance if forward else -distance
        )
        got_state = got_state.astype(jnp.float32)
        near_state = near_state + near_decay[:, None] * got_state
        near_decay = near_decay * got_decay
        if distance * 2 < size:
            far_state = far_state + far_decay[:, None] * got_state
            far_decay = far_decay * got_decay
        distance *= 2
    return near_state


def shards(bwd_input, bwd_docs, bwd_grad, proj_weight, step_weight, step_bias, rate_log, skip_gain):
    tokens = bwd_input.shape[1]
    channels_here = bwd_input.shape[2]
    heads_here = step_bias.shape[1]
    head_width = channels_here // heads_here
    bwd_flat = bwd_input[0]
    bwd_values = bwd_flat.reshape(tokens, heads_here, head_width)
    weight_heads = step_weight[0].reshape(heads_here, head_width)
    bias_heads = step_bias[0]
    rate_heads = rate_log[0]
    skip_heads = skip_gain[0]
    docs_bwd = bwd_docs[0]
    doc_before = shifted(docs_bwd[-1:], "seq", 1)[0]
    full_weight = lax.all_gather(proj_weight[0], "seq", axis=0, tiled=True)
    partial_value = jnp.dot(bwd_flat, full_weight.T, preferred_element_type=jnp.float32)
    mixer_bwd = lax.psum_scatter(
        partial_value.astype(jnp.bfloat16), "head", scatter_dimension=1, tiled=True
    )
    cotangent = bwd_grad[0].reshape(tokens, heads_here, head_width)

    def summary_bwd(values_in, mixer_in, weight_in, bias_in, rate_in):
        return span_summary(values_in, mixer_in, weight_in, bias_in, rate_in, docs_bwd, doc_before)

    summary_out, summary_pull = jax.vjp(
        summary_bwd, bwd_values, mixer_bwd, weight_heads, bias_heads, rate_heads
    )
    decay_bwd, state_bwd = summary_out
    state_shape = state_bwd.shape
    state_flat = state_bwd.reshape(heads_here, -1)

    def output_bwd(values_in, mixer_in, weight_in, bias_in, rate_in, skip_in, state_in):
        return span_output(
            values_in,
            mixer_in,
            weight_in,
            bias_in,
            rate_in,
            skip_in,
            docs_bwd,
            doc_before,
            state_in,
        )

    def carried_only(state_in):
        return output_bwd(
            bwd_values, mixer_bwd, weight_heads, bias_heads, rate_heads, skip_heads, state_in
        )

    state_grad = jax.vjp(carried_only, jnp.zeros(state_shape, jnp.float32))[1](cotangent)[0]
    state_grad = state_grad.reshape(heads_here, -1)
    incoming_flat = scan_rounds(decay_bwd, state_flat, "seq", True)
    adjoint_flat = scan_rounds(decay_bwd, state_grad, "seq", False)
    incoming_bwd = incoming_flat.reshape(state_shape)
    unused, output_pull = jax.vjp(
        output_bwd,
        bwd_values,
        mixer_bwd,
        weight_heads,
        bias_heads,
        rate_heads,
        skip_heads,
        incoming_bwd,
    )
    out_grads = output_pull(cotangent)
    decay_grad = jnp.sum(adjoint_flat * incoming_flat, axis=1)
    sum_grads = summary_pull((decay_grad, adjoint_flat.reshape(state_shape)))
    mixer_grad = (out_grads[1].astype(jnp.float32) + sum_grads[1].astype(jnp.float32)).astype(
        jnp.bfloat16
    )
    mixer_full = lax.all_gather(mixer_grad, "head", axis=1, tiled=True)
    back_proj = jnp.dot(mixer_full, full_weight, preferred_element_type=jnp.float32)
    value_grad = (out_grads[0].astype(jnp.float32) + sum_grads[0].astype(jnp.float32)).reshape(
        tokens, channels_here
    ) + back_proj
    value_grad = value_grad.astype(jnp.bfloat16)
    prev_part = shifted(value_grad.reshape(1, tokens, channels_here), "section", -1)
    grad_rows = lax.psum_scatter(
        lax.dot_general(
            mixer_full, bwd_flat, (((0,), (0,)), ((), ())), preferred_element_type=jnp.float32
        ).astype(jnp.bfloat16),
        "seq",
        scatter_dimension=0,
        tiled=True,
    ).astype(jnp.float32)
    totals = lax.psum(
        (
            (out_grads[2] + sum_grads[2]).reshape(channels_here),
            out_grads[3] + sum_grads[3],
            out_grads[4] + sum_grads[4],
            out_grads[5],
        ),
        "seq",
    )
    return (
        prev_part,
        grad_rows[None],
        totals[0][None],
        totals[1][None],
        totals[2][None],
        totals[3][None],
    )


def solution(mesh):
    in_specs = (
        P("section", "seq", "head"),
        P("section", "seq"),
        P("section", "seq", "head"),
        P("section", "seq", "head"),
        P("section", "head"),
        P("section", "head"),
        P("section", "head"),
        P("section", "head"),
    )
    out_specs = (
        P("section", "seq", "head"),
        P("section", "seq", "head"),
        P("section", "head"),
        P("section", "head"),
        P("section", "head"),
        P("section", "head"),
    )
    return jax.shard_map(shards, mesh=mesh, in_specs=in_specs, out_specs=out_specs, check_vma=False)
```

profile of v0, /device:TPU:0, one launch (start us, length us, event | category | flops | bytes accessed | tf_op | source)
XLA Modules:
  0.0 210.8 jit_solution(10798965876663877636)
XLA Ops:
  8.5 5.4 %collective-permute-start.1 = (s32[1]{0:T(128)}, s32[1]{0:T(128)}, u32[]{:S(2)}, u32[]{:S(2)}) collective-permute-start(s32[1]{0:T(128)} %bitcast.18), channel_id=1, source_target_pairs={{0,2},{2,4},{4,6},{6,8},{8,10},{10,12},{12,14},{1,3},{3,5},{5,7},{... | collective-permute-start | bytes 20 | tf_op jit(solution)/shard_map/ppermute | solution.py:12
  13.9 32.6 %all-gather = bf16[1,256,1792]{2,1,0:T(8,128)(2,1)S(1)} all-gather(bf16[1,32,1792]{2,1,0:T(8,128)(2,1)} %param.12), channel_id=2, replica_groups=mesh['section'=2,'seq'=8,'head'=2] {'seq'}, dimensions={1}, use_global_device_ids=true | all-gather | bytes 1032192 | tf_op jit(solution)/shard_map/all_gather | solution.py:117
  54.9 1.4 fusion.37
  56.2 1.5 reshape.210
  58.5 4.3 %collective-permute-start = (bf16[28,4096]{1,0:T(8,128)(2,1)}, bf16[28,4096]{1,0:T(8,128)(2,1)}, u32[]{:S(2)}, u32[]{:S(2)}) collective-permute-start(bf16[28,4096]{1,0:T(8,128)(2,1)} %convert_element_type.189), channel_id=1, source_target_pairs={{0,2},{2,4},{4,6},{6,8},{8,10},{10,12},{12,14},{1,3},{3,5},{5,7},{... | collective-permute-start | bytes 688136 | tf_op jit(solution)/shard_map/ppermute | solution.py:12
  62.8 1.6 convolution_bitcast_fusion
  64.4 2.4 %copy.93 = f32[28,64,64]{2,1,0:T(8,128)} copy(f32[28,64,64]{1,2,0:T(8,128)} %convolution_bitcast_fusion) | data formatting | bytes 917504 | tf_op jit(solution)/shard_map/transpose(jvp(tn,hnp->thp))/transpose | solution.py:75
  66.8 1.5 reshape.212
  68.3 1.3 collective-permute-start.6
  70.7 4.8 %collective-permute-start.3 = (bf16[28,4096]{1,0:T(8,128)(2,1)S(1)}, bf16[28,4096]{1,0:T(8,128)(2,1)S(1)}, u32[]{:S(2)}, u32[]{:S(2)}) collective-permute-start(bf16[28,4096]{1,0:T(8,128)(2,1)S(1)} %fusion.56), channel_id=1, source_target_pairs={{0,4},{2,6},{4,8},{6,10},{8,12},{10,14},{1,5},{3,7},{5,9},{7,11},{... | collective-permute-start | bytes 688136 | tf_op jit(solution)/shard_map/ppermute | solution.py:12
  75.6 2.5 %collective-permute-start.2 = (f32[28]{0:T(128)S(1)}, f32[28]{0:T(128)S(1)}, u32[]{:S(2)}, u32[]{:S(2)}) collective-permute-start(f32[28]{0:T(128)S(1)} %copy-done.36), channel_id=1, source_target_pairs={{0,2},{2,4},{4,6},{6,8},{8,10},{10,12},{12,14},{1,3},{3,5},{5,7},{... | collective-permute-start | bytes 344 | tf_op jit(solution)/shard_map/ppermute | solution.py:12
  79.4 4.5 %collective-permute-done.7 = f32[28]{0:T(128)S(1)} collective-permute-done((f32[28]{0:T(128)S(1)}, f32[28]{0:T(128)S(1)}, u32[]{:S(2)}, u32[]{:S(2)}) %collective-permute-start.7) | collective-permute-done | bytes 144 | tf_op jit(solution)/shard_map/ppermute | solution.py:12
  84.3 2.0 fusion.41
  86.4 1.4 collective-permute-start.8
  88.5 5.5 %collective-permute-start.5 = (bf16[28,4096]{1,0:T(8,128)(2,1)}, bf16[28,4096]{1,0:T(8,128)(2,1)S(1)}, u32[]{:S(2)}, u32[]{:S(2)}) collective-permute-start(bf16[28,4096]{1,0:T(8,128)(2,1)} %get-tuple-element.40), channel_id=1, source_target_pairs={{0,8},{2,10},{4,12},{6,14},{1,9},{3,11},{5,13},{7,15},{16,24},{18,... | collective-permute-start | bytes 688136 | tf_op jit(solution)/shard_map/ppermute | solution.py:12
  97.7 1.4 reshape_squeeze.10
  99.1 2.6 %fusion.25 = (f32[1792]{0:T(1024)}, f32[1,128,1792]{1,2,0:T(8,128)}) fusion(bf16[1,128,1792]{1,2,0:T(8,128)(2,1)S(1)} %copy.81, bf16[1,128,1792]{1,2,0:T(8,128)(2,1)S(1)} %copy.82, f32[128,28]{0,1:T(8,128)} %copy-done.12), kind=kLoop, calls=%fused_computation.45 | loop fusion | flops 1145088 | bytes 1856512 | tf_op jit(solution)/shard_map/transpose(jvp())/reduce_sum | solution.py:77
  101.6 1.4 reduce_sum.160
  103.0 4.0 %collective-permute-start.4 = (f32[28]{0:T(128)}, f32[28]{0:T(128)}, u32[]{:S(2)}, u32[]{:S(2)}) collective-permute-start(f32[28]{0:T(128)} %copy-done.49), channel_id=1, source_target_pairs={{0,4},{2,6},{4,8},{6,10},{8,12},{10,14},{1,5},{3,7},{5,9},{7,11},{... | collective-permute-start | bytes 344 | tf_op jit(solution)/shard_map/ppermute | solution.py:12
  107.0 1.4 reduce_sum.161
  110.3 4.3 %collective-permute-done.9 = f32[28]{0:T(128)S(1)} collective-permute-done((f32[28]{0:T(128)}, f32[28]{0:T(128)S(1)}, u32[]{:S(2)}, u32[]{:S(2)}) %collective-permute-start.9) | collective-permute-done | bytes 144 | tf_op jit(solution)/shard_map/ppermute | solution.py:12
  116.8 2.9 %multiply_reduce_fusion.2 = (f32[28]{0:T(128)}, bf16[28,4096]{1,0:T(8,128)(2,1)S(1)}, f32[28,4096]{1,0:T(8,128)}) fusion(bf16[28,4096]{1,0:T(8,128)(2,1)} %collective-permute-done.10, f32[28]{0:T(128)S(1)} %mul.365, bf16[28,4096]{1,0:T(8,128)(2,1)S(1)} %collective-permute-done.8, f32[28]{0:T(128)} %copy-done.46, bf16[28,4096]{1,0:T(8,128)(2,1)S(1)} %copy-done.2, ...), kind=kLoop, calls=%fused_computation.79 | loop fusion | flops 1949668 | bytes 2064944 | tf_op jit(solution)/shard_map/reduce_sum | solution.py:168
  122.4 2.5 %fusion.12 = (f32[28,128]{1,0:T(8,128)}, f32[28,128]{1,0:T(8,128)}, f32[28,128]{1,0:T(8,128)S(1)}, bf16[128,128]{1,0:T(8,128)(2,1)S(1)}) fusion(f32[28,128]{1,0:T(8,128)S(1)} %copy.85, f32[128,128]{1,0:T(8,128)S(1)} %copy-done.15, f32[128,128]{1,0:T(8,128)S(1)} %copy-done.17, f32[28,128]{1,0:T(8,128)S(1)} %bitcast.243, pred[128,128]{1,0:T(8,128)(4,1)S(1)} %copy-done.25, ...), kind=kOutput, calls=%fused_computation.19 | convolution fusion | flops 66491904 | bytes 1169408 | tf_op jit(solution)/shard_map/transpose(jvp(hts,shp->thp))/dot_general | solution.py:16
  125.2 1.4 reshape.211
  127.8 1.7 fusion.87
  131.1 2.2 %fusion.24 = bf16[128,64]{0,1:T(8,128)(2,1)S(1)} fusion(bf16[128,64]{0,1:T(8,128)(2,1)S(1)} %convolution_convert_fusion.7, f32[128,28,64]{0,2,1:T(8,128)} %bitcast.228, f32[28,64,64]{2,1,0:T(8,128)S(1)} %reshape.211), kind=kOutput, calls=%fused_computation.44 | convolution fusion | flops 176177152 | bytes 1409024 | tf_op jit(solution)/shard_map/transpose(jvp(tn,hnp->thp))/dot_general | solution.py:75
  133.2 2.0 all_gather.7
  135.4 1.4 convolution_convert_fusion
  140.6 1.4 collective-permute-start.11
  143.9 22.8 %all-reduce.4 = (f32[1,1792]{1,0:T(1,128)}, f32[1,28]{1,0:T(1,128)}, f32[1,28]{1,0:T(1,128)}, f32[1,28]{1,0:T(1,128)}) all-reduce(f32[1,1792]{1,0:T(1,128)S(1)} %broadcast_in_dim.47, f32[1,28]{1,0:T(1,128)S(1)} %get-tuple-element.50, f32[1,28]{1,0:T(1,128)S(1)} %get-tuple-element.49, ...), channel_id=1, replica_groups=mesh['section'=2,'seq'=8,'head'=2] {'seq'}, use_global_device_ids=true, to_apply=%region_11.13 | all-reduce | flops 1876 | bytes 15008 | tf_op jit(solution)/shard_map/psum | solution.py:188
  166.7 34.9 %reduce-scatter.5.cloned.1.call-done = bf16[32,1792]{1,0:T(8,128)(2,1)} async-done(((bf16[256,1792]{1,0:T(8,128)(2,1)}), bf16[32,1792]{1,0:T(8,128)(2,1)}) %reduce-scatter.5.cloned.1.call-update) | async-done | bytes 114704 | tf_op jit(solution)/shard_map/reduce_scatter | solution.py:180
  201.6 1.6 bitcast_convert_fusion
  (202 shorter events, 32.0 us)
Async XLA Ops:
  7.2 39.4 %copy-start = (bf16[1,128,1792]{2,1,0:T(8,128)(2,1)S(1)}, bf16[1,128,1792]{2,1,0:T(8,128)(2,1)}, u32[]{:S(2)}) copy-start(bf16[1,128,1792]{2,1,0:T(8,128)(2,1)} %param.9) | copy-start | bytes 1376260
  7.2 47.0 %reduce-scatter.7.cloned.1.call-start = ((), (), s32[]{:S(2)}) async-start(), calls=%async_computation.3 | async-start | bytes 98304
  8.5 40.6 %collective-permute-start.1 = (s32[1]{0:T(128)}, s32[1]{0:T(128)}, u32[]{:S(2)}, u32[]{:S(2)}) collective-permute-start(s32[1]{0:T(128)} %bitcast.18), channel_id=1, source_target_pairs={{0,2},{2,4},{4,6},{6,8},{8,10},{10,12},{12,14},{1,3},{3,5},{5,7},{... | collective-permute-start | bytes 20 | tf_op jit(solution)/shard_map/ppermute | solution.py:12
  47.8 153.8 %reduce-scatter.5.cloned.1.call-start = ((), (), s32[]{:S(2)}) async-start(), calls=%async_computation.2 | async-start | bytes 1032192 | tf_op jit(solution)/shard_map/reduce_scatter | solution.py:180
  48.1 3.6 %copy-start.37 = (f32[1,28]{1,0:T(1,128)S(1)}, f32[1,28]{1,0:T(1,128)}, u32[]{:S(2)}) copy-start(f32[1,28]{1,0:T(1,128)} %param.14) | copy-start | bytes 340
  48.9 7.3 %copy-start.59 = (f32[28]{0:T(128)}, f32[28]{0:T(128)S(1)}, u32[]{:S(2)}) copy-start(f32[28]{0:T(128)S(1)} %negate_bitcast_fusion) | copy-start | bytes 340
  50.5 5.8 %copy-start.28 = (pred[128]{0:T(512)(128)(4,1)}, pred[128]{0:T(512)(128)(4,1)S(1)}, u32[]{:S(2)}) copy-start(pred[128]{0:T(512)(128)(4,1)S(1)} %get-tuple-element.31) | copy-start | bytes 388
  50.5 5.7 %copy-start.31 = (f32[128]{0:T(128)}, f32[128]{0:T(128)S(1)}, u32[]{:S(2)}) copy-start(f32[128]{0:T(128)S(1)} %get-tuple-element.32) | copy-start | bytes 1540
  52.0 10.8 %copy-start.12 = (f32[128,28]{0,1:T(8,128)}, f32[128,28]{0,1:T(8,128)S(1)}, u32[]{:S(2)}) copy-start(f32[128,28]{0,1:T(8,128)S(1)} %get-tuple-element.47) | copy-start | bytes 43012
  52.2 5.6 %copy-start.40 = (f32[28]{0:T(128)}, f32[28]{0:T(128)S(1)}, u32[]{:S(2)}) copy-start(f32[28]{0:T(128)S(1)} %slice_bitcast_fusion) | copy-start | bytes 340
  56.2 6.6 %copy-start.8 = (bf16[128,128]{1,0:T(8,128)(2,1)S(1)}, bf16[128,128]{1,0:T(8,128)(2,1)}, u32[]{:S(2)}) copy-start(bf16[128,128]{1,0:T(8,128)(2,1)} %reduce-scatter.7.cloned.1.call-done) | copy-start | bytes 98308
  58.5 11.2 %collective-permute-start = (bf16[28,4096]{1,0:T(8,128)(2,1)}, bf16[28,4096]{1,0:T(8,128)(2,1)}, u32[]{:S(2)}, u32[]{:S(2)}) collective-permute-start(bf16[28,4096]{1,0:T(8,128)(2,1)} %convert_element_type.189), channel_id=1, source_target_pairs={{0,2},{2,4},{4,6},{6,8},{8,10},{10,12},{12,14},{1,3},{3,5},{5,7},{... | collective-permute-start | bytes 688136 | tf_op jit(solution)/shard_map/ppermute | solution.py:12
  68.3 7.3 %copy-start.36 = (f32[28]{0:T(128)S(1)}, f32[28]{0:T(128)}, u32[]{:S(2)}) copy-start(f32[28]{0:T(128)} %exponential_multiply_fusion.1) | copy-start | bytes 340
  68.3 15.5 %collective-permute-start.6 = (bf16[28,4096]{1,0:T(8,128)(2,1)S(1)}, bf16[28,4096]{1,0:T(8,128)(2,1)S(1)}, u32[]{:S(2)}, u32[]{:S(2)}) collective-permute-start(bf16[28,4096]{1,0:T(8,128)(2,1)S(1)} %convert_element_type.200), channel_id=1, source_target_pairs={{2,0},{4,2},{6,4},{8,6},{10,8},{12,10},{14,12},{3,1},{5,3},{7,5},{... | collective-permute-start | bytes 688136 | tf_op jit(solution)/shard_map/ppermute | solution.py:12
  70.7 13.2 %collective-permute-start.3 = (bf16[28,4096]{1,0:T(8,128)(2,1)S(1)}, bf16[28,4096]{1,0:T(8,128)(2,1)S(1)}, u32[]{:S(2)}, u32[]{:S(2)}) collective-permute-start(bf16[28,4096]{1,0:T(8,128)(2,1)S(1)} %fusion.56), channel_id=1, source_target_pairs={{0,4},{2,6},{4,8},{6,10},{8,12},{10,14},{1,5},{3,7},{5,9},{7,11},{... | collective-permute-start | bytes 688136 | tf_op jit(solution)/shard_map/ppermute | solution.py:12
  75.6 3.8 %collective-permute-start.2 = (f32[28]{0:T(128)S(1)}, f32[28]{0:T(128)S(1)}, u32[]{:S(2)}, u32[]{:S(2)}) collective-permute-start(f32[28]{0:T(128)S(1)} %copy-done.36), channel_id=1, source_target_pairs={{0,2},{2,4},{4,6},{6,8},{8,10},{10,12},{12,14},{1,3},{3,5},{5,7},{... | collective-permute-start | bytes 344 | tf_op jit(solution)/shard_map/ppermute | solution.py:12
  78.0 5.8 %collective-permute-start.7 = (f32[28]{0:T(128)S(1)}, f32[28]{0:T(128)S(1)}, u32[]{:S(2)}, u32[]{:S(2)}) collective-permute-start(f32[28]{0:T(128)S(1)} %copy-done.36), channel_id=1, source_target_pairs={{2,0},{4,2},{6,4},{8,6},{10,8},{12,10},{14,12},{3,1},{5,3},{7,5},{... | collective-permute-start | bytes 344 | tf_op jit(solution)/shard_map/ppermute | solution.py:12
  79.4 4.5 %copy-start.45 = (f32[28]{0:T(128)}, f32[28]{0:T(128)S(1)}, u32[]{:S(2)}) copy-start(f32[28]{0:T(128)S(1)} %collective-permute-done.2) | copy-start | bytes 340
  83.9 11.1 %copy-start.47 = (f32[28]{0:T(128)}, f32[28]{0:T(128)S(1)}, u32[]{:S(2)}) copy-start(f32[28]{0:T(128)S(1)} %get-tuple-element.43) | copy-start | bytes 340
  83.9 11.0 %copy-start.1 = (bf16[28,4096]{1,0:T(8,128)(2,1)}, bf16[28,4096]{1,0:T(8,128)(2,1)S(1)}, u32[]{:S(2)}) copy-start(bf16[28,4096]{1,0:T(8,128)(2,1)S(1)} %collective-permute-done.6) | copy-start | bytes 688132
  84.3 3.4 %copy-start.35 = (s32[1,128]{1,0:T(1,128)S(1)}, s32[1,128]{1,0:T(1,128)}, u32[]{:S(2)}) copy-start(s32[1,128]{1,0:T(1,128)} %param.10) | copy-start | bytes 1540
  86.4 10.7 %copy-start.58 = (f32[1,28]{1,0:T(1,128)S(1)}, f32[1,28]{1,0:T(1,128)}, u32[]{:S(2)}) copy-start(f32[1,28]{1,0:T(1,128)} %param.16) | copy-start | bytes 340
  86.4 8.6 %collective-permute-start.8 = (bf16[28,4096]{1,0:T(8,128)(2,1)S(1)}, bf16[28,4096]{1,0:T(8,128)(2,1)S(1)}, u32[]{:S(2)}, u32[]{:S(2)}) collective-permute-start(bf16[28,4096]{1,0:T(8,128)(2,1)S(1)} %get-tuple-element.41), channel_id=1, source_target_pairs={{4,0},{6,2},{8,4},{10,6},{12,8},{14,10},{5,1},{7,3},{9,5},{11,7},{... | collective-permute-start | bytes 688136 | tf_op jit(solution)/shard_map/ppermute | solution.py:12
  88.5 27.6 %collective-permute-start.5 = (bf16[28,4096]{1,0:T(8,128)(2,1)}, bf16[28,4096]{1,0:T(8,128)(2,1)S(1)}, u32[]{:S(2)}, u32[]{:S(2)}) collective-permute-start(bf16[28,4096]{1,0:T(8,128)(2,1)} %get-tuple-element.40), channel_id=1, source_target_pairs={{0,8},{2,10},{4,12},{6,14},{1,9},{3,11},{5,13},{7,15},{16,24},{18,... | collective-permute-start | bytes 688136 | tf_op jit(solution)/shard_map/ppermute | solution.py:12
  95.8 21.0 %collective-permute-start.10 = (bf16[28,4096]{1,0:T(8,128)(2,1)}, bf16[28,4096]{1,0:T(8,128)(2,1)}, u32[]{:S(2)}, u32[]{:S(2)}) collective-permute-start(bf16[28,4096]{1,0:T(8,128)(2,1)} %fusion.45), channel_id=1, source_target_pairs={{8,0},{10,2},{12,4},{14,6},{9,1},{11,3},{13,5},{15,7},{24,16},{26,... | collective-permute-start | bytes 688136 | tf_op jit(solution)/shard_map/ppermute | solution.py:12
  99.0 17.8 %copy-start.2 = (bf16[28,4096]{1,0:T(8,128)(2,1)S(1)}, bf16[28,4096]{1,0:T(8,128)(2,1)}, u32[]{:S(2)}) copy-start(bf16[28,4096]{1,0:T(8,128)(2,1)} %copy-done.1) | copy-start | bytes 688132
  99.1 17.8 %copy-start.6 = (bf16[28,4096]{1,0:T(8,128)(2,1)S(1)}, bf16[28,4096]{1,0:T(8,128)(2,1)}, u32[]{:S(2)}) copy-start(bf16[28,4096]{1,0:T(8,128)(2,1)} %copy-done.5) | copy-start | bytes 688132
  103.0 6.6 %collective-permute-start.4 = (f32[28]{0:T(128)}, f32[28]{0:T(128)}, u32[]{:S(2)}, u32[]{:S(2)}) collective-permute-start(f32[28]{0:T(128)} %copy-done.49), channel_id=1, source_target_pairs={{0,4},{2,6},{4,8},{6,10},{8,12},{10,14},{1,5},{3,7},{5,9},{7,11},{... | collective-permute-start | bytes 344 | tf_op jit(solution)/shard_map/ppermute | solution.py:12
  108.3 6.3 %collective-permute-start.9 = (f32[28]{0:T(128)}, f32[28]{0:T(128)S(1)}, u32[]{:S(2)}, u32[]{:S(2)}) collective-permute-start(f32[28]{0:T(128)} %copy-done.47), channel_id=1, source_target_pairs={{4,0},{6,2},{8,4},{10,6},{12,8},{14,10},{5,1},{7,3},{9,5},{11,7},{... | collective-permute-start | bytes 344 | tf_op jit(solution)/shard_map/ppermute | solution.py:12
  140.5 3.2 %copy-start.51 = (f32[1,28]{1,0:T(1,128)S(1)}, f32[1,28]{1,0:T(1,128)}, u32[]{:S(2)}) copy-start(f32[1,28]{1,0:T(1,128)} %param.15) | copy-start | bytes 340
  140.6 3.2 %copy-start.48 = (f32[28]{0:T(128)S(1)}, f32[28]{0:T(128)}, u32[]{:S(2)}) copy-start(f32[28]{0:T(128)} %reduce_sum.161) | copy-start | bytes 340
  140.6 26.1 %collective-permute-start.11 = (bf16[1,128,1792]{2,1,0:T(8,128)(2,1)S(1)}, bf16[1,128,1792]{2,1,0:T(8,128)(2,1)S(1)}, u32[]{:S(2)}, u32[]{:S(2)}) collective-permute-start(bf16[1,128,1792]{2,1,0:T(8,128)(2,1)S(1)} %fusion.1), channel_id=1, source_target_pairs={{16,0},{17,1},{18,2},{19,3},{20,4},{21,5},{22,6},{23,7},{24,8},{25... | collective-permute-start | bytes 1376264 | tf_op jit(solution)/shard_map/ppermute | solution.py:12
  (46 other events, 79.0 us)
Sparse Core Ops, SparseCore 0:
  47.9 6.1 reduce-scatter.6
  136.9 64.6 reduce-scatter.4
where the time goes:
time: 212 us; the launch traced here: 211 us
  blocking collectives  57.5 us (27%)
  waiting for transfers between devices  45.5 us (21%)
  starting transfers between devices  34.5 us (16%)
  other arithmetic  20.5 us (10%)
  local copies, waits for them, and re-layouts  18.9 us (9%)
  matrix products  17.6 us (8%)
  between operations  16.3 us (8%)
    reduce_scatter x1, waiting for transfers between devices, shards(): lax.psum_scatter(lax.dot_general(mixer_full, bwd_flat, (((0,), (0,)), (()...  34.9 us
    ppermute x12, starting transfers between devices, shifted(): return lax.ppermute(block, axis, route)  34.4 us
    all_gather x1, blocking collectives, shards(): full_weight = lax.all_gather(proj_weight[0], 'seq', axis=0, tiled=True)  32.6 us
    psum x1, blocking collectives, shards(): lax.psum(((out_grads[2] + sum_grads[2]).reshape(channels_here), out_grads...  22.8 us
    ppermute x12, waiting for transfers between devices, shifted(): return lax.ppermute(block, axis, route)  9.77 us
    dot_general x5, matrix products, contract(): return jnp.einsum(spec, left, right, preferred_element_type=jnp.float32)  5.53 us
    convert_element_type x5, other arithmetic, scan_rounds(): far_state.astype(jnp.bfloat16)  4.74 us
    unnamed x132, local copies, waits for them, and re-layouts  4.31 us
  transfers between devices with their start and end apart: 14, of which 5 were waited for; matrix products, arithmetic and copies ran while one was open for 13% of the time, Pallas kernels for 0%

commit v1 on v0

--- a/solution.py
+++ b/solution.py
@@ -114,7 +114,12 @@
     skip_heads = skip_gain[0]
     docs_bwd = bwd_docs[0]
     doc_before = shifted(docs_bwd[-1:], "seq", 1)[0]
-    full_weight = lax.all_gather(proj_weight[0], "seq", axis=0, tiled=True)
+    ring = [proj_weight[0]]
+    for hop in range(7):
+        ring.append(lax.ppermute(ring[-1], "seq", [(dev, (dev + 1) % 8) for dev in range(8)]))
+    full_weight = jnp.roll(
+        jnp.concatenate(ring[::-1], axis=0), (lax.axis_index("seq") + 1) * ring[0].shape[0], axis=0
+    )
     partial_value = jnp.dot(bwd_flat, full_weight.T, preferred_element_type=jnp.float32)
     mixer_bwd = lax.psum_scatter(
         partial_value.astype(jnp.bfloat16), "head", scatter_dimension=1, tiled=True

time: 212 us -> 230 us (1.085)
  waiting for transfers between devices: 45.5 us -> 87.7 us
  blocking collectives: 57.5 us -> 23 us
  starting transfers between devices: 34.5 us -> 41.3 us
  local copies, waits for them, and re-layouts: 18.9 us -> 23.6 us
  other arithmetic: 20.5 us -> 16.6 us
  matrix products: 17.6 us -> 20.4 us
    ppermute x0 -> x7, waiting for transfers between devices: none -> 40.9 us  [shards(): lax.ppermute(ring[-1], 'seq', [(dev, (dev + 1) % 8) for dev in range(8)])]
    all_gather x1 -> x0, blocking collectives: 32.6 us -> none  [shards(): full_weight = lax.all_gather(proj_weight[0], 'seq', axis=0, tiled=True)]
    unnamed x132 -> x106, local copies, waits for them, and re-layouts: 4.31 us -> 12.4 us
    reduce_scatter x0 -> x1, waiting for transfers between devices: none -> 4.8 us  [shards(): lax.psum_scatter(partial_value.astype(jnp.bfloat16), 'head', scatter_dime...]
    ppermute x0 -> x7, starting transfers between devices: none -> 4.04 us  [shards(): lax.ppermute(ring[-1], 'seq', [(dev, (dev + 1) % 8) for dev in range(8)])]
    reduce_sum x2, other arithmetic: 3.95 us -> 0.94 us  [span_output(): values.astype(jnp.float32) * (1.0 + skip_gain)[None, :, None] + local_part]
    ppermute x12, starting transfers between devices: 34.4 us -> 37.2 us  [shifted(): return lax.ppermute(block, axis, route)]
  transfers between devices with their start and end apart: 14 -> 21, of which waited for: 5 -> 11; matrix products, arithmetic and copies ran while one was open for 13% -> 9% of each run, Pallas kernels for 0% -> 0%
where the time goes in v1:
time: 230 us; the launch traced here: 229 us
  waiting for transfers between devices  87.7 us (38%)
  starting transfers between devices  41.3 us (18%)
  local copies, waits for them, and re-layouts  23.6 us (10%)
  blocking collectives  23 us (10%)
  matrix products  20.4 us (9%)
  other arithmetic  16.6 us (7%)
  between operations  16.1 us (7%)
    ppermute x7, waiting for transfers between devices, shards(): lax.ppermute(ring[-1], 'seq', [(dev, (dev + 1) % 8) for dev in range(8)])  40.9 us
    ppermute x12, starting transfers between devices, shifted(): return lax.ppermute(block, axis, route)  37.2 us
    reduce_scatter x1, waiting for transfers between devices, shards(): lax.psum_scatter(lax.dot_general(mixer_full, bwd_flat, (((0,), (0,)), (()...  34.3 us
    psum x1, blocking collectives, shards(): lax.psum(((out_grads[2] + sum_grads[2]).reshape(channels_here), out_grads...  20.9 us
    unnamed x106, local copies, waits for them, and re-layouts  12.4 us
    ppermute x12, waiting for transfers between devices, shifted(): return lax.ppermute(block, axis, route)  7.63 us
    dot_general x5, matrix products, contract(): return jnp.einsum(spec, left, right, preferred_element_type=jnp.float32)  7.11 us
    reduce_scatter x1, waiting for transfers between devices, shards(): lax.psum_scatter(partial_value.astype(jnp.bfloat16), 'head', scatter_dime...  4.8 us
  transfers between devices with their start and end apart: 21, of which 11 were waited for; matrix products, arithmetic and copies ran while one was open for 9% of the time, Pallas kernels for 0%

profile of v1, /device:TPU:0, one launch (start us, length us, event | category | flops | bytes accessed | tf_op | source)
XLA Modules:
  0.0 228.7 jit_solution(17712118612576838941)
XLA Ops:
  7.3 3.0 %collective-permute-start = (bf16[32,1792]{1,0:T(8,128)(2,1)}, bf16[32,1792]{1,0:T(8,128)(2,1)S(1)}, u32[]{:S(2)}, u32[]{:S(2)}) collective-permute-start(bf16[32,1792]{1,0:T(8,128)(2,1)} %bitcast.230), channel_id=1, source_target_pairs={{0,2},{2,4},{4,6},{6,8},{8,10},{10,12},{12,14},{14,0},{1,3},{3,5},... | collective-permute-start | bytes 344072 | tf_op jit(solution)/shard_map/ppermute | solution.py:119
  11.5 4.0 %collective-permute-start.8 = (s32[1]{0:T(128)}, s32[1]{0:T(128)}, u32[]{:S(2)}, u32[]{:S(2)}) collective-permute-start(s32[1]{0:T(128)} %bitcast.19), channel_id=1, source_target_pairs={{0,2},{2,4},{4,6},{6,8},{8,10},{10,12},{12,14},{1,3},{3,5},{5,7},{... | collective-permute-start | bytes 20 | tf_op jit(solution)/shard_map/ppermute | solution.py:12
  19.5 5.7 %collective-permute-done.1 = bf16[32,1792]{1,0:T(8,128)(2,1)S(1)} collective-permute-done((bf16[32,1792]{1,0:T(8,128)(2,1)S(1)}, bf16[32,1792]{1,0:T(8,128)(2,1)S(1)}, u32[]{:S(2)}, u32[]{:S(2)}) %collective-permute-start.1) | collective-permute-done | bytes 114720 | tf_op jit(solution)/shard_map/ppermute | solution.py:119
  25.2 7.5 %collective-permute-done.2 = bf16[32,1792]{1,0:T(8,128)(2,1)S(1)} collective-permute-done((bf16[32,1792]{1,0:T(8,128)(2,1)S(1)}, bf16[32,1792]{1,0:T(8,128)(2,1)S(1)}, u32[]{:S(2)}, u32[]{:S(2)}) %collective-permute-start.2) | collective-permute-done | bytes 114720 | tf_op jit(solution)/shard_map/ppermute | solution.py:119
  32.6 1.3 broadcast_compare_fusion.1
  34.0 6.1 %collective-permute-done.3 = bf16[32,1792]{1,0:T(8,128)(2,1)S(1)} collective-permute-done((bf16[32,1792]{1,0:T(8,128)(2,1)S(1)}, bf16[32,1792]{1,0:T(8,128)(2,1)S(1)}, u32[]{:S(2)}, u32[]{:S(2)}) %collective-permute-start.3) | collective-permute-done | bytes 114720 | tf_op jit(solution)/shard_map/ppermute | solution.py:119
  40.5 7.1 %collective-permute-done.4 = bf16[32,1792]{1,0:T(8,128)(2,1)S(1)} collective-permute-done((bf16[32,1792]{1,0:T(8,128)(2,1)S(1)}, bf16[32,1792]{1,0:T(8,128)(2,1)S(1)}, u32[]{:S(2)}, u32[]{:S(2)}) %collective-permute-start.4) | collective-permute-done | bytes 114720 | tf_op jit(solution)/shard_map/ppermute | solution.py:119
  47.6 8.6 %collective-permute-done.5 = bf16[32,1792]{1,0:T(8,128)(2,1)S(1)} collective-permute-done((bf16[32,1792]{1,0:T(8,128)(2,1)S(1)}, bf16[32,1792]{1,0:T(8,128)(2,1)S(1)}, u32[]{:S(2)}, u32[]{:S(2)}) %collective-permute-start.5) | collective-permute-done | bytes 114720 | tf_op jit(solution)/shard_map/ppermute | solution.py:119
  57.8 6.0 %collective-permute-done.6 = bf16[32,1792]{1,0:T(8,128)(2,1)S(1)} collective-permute-done((bf16[32,1792]{1,0:T(8,128)(2,1)S(1)}, bf16[32,1792]{1,0:T(8,128)(2,1)S(1)}, u32[]{:S(2)}, u32[]{:S(2)}) %collective-permute-start.6) | collective-permute-done | bytes 114720 | tf_op jit(solution)/shard_map/ppermute | solution.py:119
  74.2 2.2 fusion.23
  76.5 4.8 %reduce-scatter.3.cloned.1.call-done = bf16[128,128]{0,1:T(8,128)(2,1)} async-done(((bf16[128,256]{0,1:T(8,128)(2,1)}), bf16[128,128]{0,1:T(8,128)(2,1)}) %reduce-scatter.3.cloned.1.call-update) | async-done | bytes 32784 | tf_op jit(solution)/shard_map/reduce_scatter | solution.py:124
  83.4 4.3 %collective-permute-start.7 = (bf16[28,4096]{1,0:T(8,128)(2,1)}, bf16[28,4096]{1,0:T(8,128)(2,1)}, u32[]{:S(2)}, u32[]{:S(2)}) collective-permute-start(bf16[28,4096]{1,0:T(8,128)(2,1)} %convert_element_type.193), channel_id=1, source_target_pairs={{0,2},{2,4},{4,6},{6,8},{8,10},{10,12},{12,14},{1,3},{3,5},{5,7},{... | collective-permute-start | bytes 688136 | tf_op jit(solution)/shard_map/ppermute | solution.py:12
  87.8 1.5 convolution_bitcast_fusion
  89.3 1.5 copy.71
  94.5 5.3 %collective-permute-start.10 = (bf16[28,4096]{1,0:T(8,128)(2,1)S(1)}, bf16[28,4096]{1,0:T(8,128)(2,1)S(1)}, u32[]{:S(2)}, u32[]{:S(2)}) collective-permute-start(bf16[28,4096]{1,0:T(8,128)(2,1)S(1)} %fusion.57), channel_id=1, source_target_pairs={{0,4},{2,6},{4,8},{6,10},{8,12},{10,14},{1,5},{3,7},{5,9},{7,11},{... | collective-permute-start | bytes 688136 | tf_op jit(solution)/shard_map/ppermute | solution.py:12
  101.1 4.5 %collective-permute-start.9 = (f32[28]{0:T(128)S(1)}, f32[28]{0:T(128)S(1)}, u32[]{:S(2)}, u32[]{:S(2)}) collective-permute-start(f32[28]{0:T(128)S(1)} %exponential_multiply_fusion.1), channel_id=1, source_target_pairs={{0,2},{2,4},{4,6},{6,8},{8,10},{10,12},{12,14},{1,3},{3,5},{5,7},{... | collective-permute-start | bytes 344 | tf_op jit(solution)/shard_map/ppermute | solution.py:12
  107.0 1.9 fusion.42
  110.9 7.8 %collective-permute-start.12 = (bf16[28,4096]{1,0:T(8,128)(2,1)}, bf16[28,4096]{1,0:T(8,128)(2,1)}, u32[]{:S(2)}, u32[]{:S(2)}) collective-permute-start(bf16[28,4096]{1,0:T(8,128)(2,1)} %get-tuple-element.40), channel_id=1, source_target_pairs={{0,8},{2,10},{4,12},{6,14},{1,9},{3,11},{5,13},{7,15},{16,24},{18,... | collective-permute-start | bytes 688136 | tf_op jit(solution)/shard_map/ppermute | solution.py:12
  122.5 3.5 %collective-permute-start.11 = (f32[28]{0:T(128)S(1)}, f32[28]{0:T(128)S(1)}, u32[]{:S(2)}, u32[]{:S(2)}) collective-permute-start(f32[28]{0:T(128)S(1)} %get-tuple-element.42), channel_id=1, source_target_pairs={{0,4},{2,6},{4,8},{6,10},{8,12},{10,14},{1,5},{3,7},{5,9},{7,11},{... | collective-permute-start | bytes 344 | tf_op jit(solution)/shard_map/ppermute | solution.py:12
  127.9 5.4 %collective-permute-done.16 = f32[28]{0:T(128)S(1)} collective-permute-done((f32[28]{0:T(128)S(1)}, f32[28]{0:T(128)S(1)}, u32[]{:S(2)}, u32[]{:S(2)}) %collective-permute-start.16) | collective-permute-done | bytes 144 | tf_op jit(solution)/shard_map/ppermute | solution.py:12
  134.1 3.0 %multiply_reduce_fusion.2 = (f32[28]{0:T(128)}, bf16[28,4096]{1,0:T(8,128)(2,1)S(1)}, f32[28,4096]{1,0:T(8,128)}) fusion(bf16[28,4096]{1,0:T(8,128)(2,1)} %collective-permute-done.17, f32[28]{0:T(128)S(1)} %mul.369, bf16[28,4096]{1,0:T(8,128)(2,1)S(1)} %collective-permute-done.15, f32[28]{0:T(128)} %copy-done.31, ...), kind=kLoop, calls=%fused_computation.80 | loop fusion | flops 1949668 | bytes 2064944 | tf_op jit(solution)/shard_map/reduce_sum | solution.py:173
  137.1 1.4 reshape.211
  139.8 1.7 fusion.88
  143.5 1.9 multiply_reduce_fusion
  145.6 1.5 fusion.103
  147.7 3.4 %fusion.12 = (f32[28,128]{1,0:T(8,128)}, f32[28,128]{1,0:T(8,128)}, f32[28,128]{1,0:T(8,128)S(1)}, bf16[128,128]{1,0:T(8,128)(2,1)S(1)}) fusion(f32[28,128]{1,0:T(8,128)} %copy.63, f32[128,128]{1,0:T(8,128)} %fusion.84, f32[128,128]{1,0:T(8,128)} %get-tuple-element.46, f32[28,128]{1,0:T(8,128)} %bitcast.235, pred[128,128]{1,0:T(8,128)(4,1)} %get-tuple-element.45, ...), kind=kOutput, calls=%fused_computation.19 | convolution fusion | flops 66491904 | bytes 1169408 | tf_op jit(solution)/shard_map/transpose(jvp(hts,shp->thp))/dot_general | solution.py:16
  153.4 2.2 all_gather.3
  155.5 1.3 convolution_convert_fusion
  159.8 1.5 fusion.1
  164.4 20.9 %all-reduce.4 = (f32[1,1792]{1,0:T(1,128)}, f32[1,28]{1,0:T(1,128)}, f32[1,28]{1,0:T(1,128)}, f32[1,28]{1,0:T(1,128)}) all-reduce(f32[1,1792]{1,0:T(1,128)S(1)} %broadcast_in_dim.47, f32[1,28]{1,0:T(1,128)S(1)} %get-tuple-element.50, f32[1,28]{1,0:T(1,128)S(1)} %get-tuple-element.49, ...), channel_id=1, replica_groups=mesh['section'=2,'seq'=8,'head'=2] {'seq'}, use_global_device_ids=true, to_apply=%region_11.13 | all-reduce | flops 1876 | bytes 15008 | tf_op jit(solution)/shard_map/psum | solution.py:193
  185.3 34.3 %reduce-scatter.5.cloned.1.call-done = bf16[32,1792]{1,0:T(8,128)(2,1)} async-done(((bf16[256,1792]{1,0:T(8,128)(2,1)}), bf16[32,1792]{1,0:T(8,128)(2,1)}) %reduce-scatter.5.cloned.1.call-update) | async-done | bytes 114704 | tf_op jit(solution)/shard_map/reduce_scatter | solution.py:185
  219.5 1.6 bitcast_convert_fusion
  (190 shorter events, 45.8 us)
Async XLA Ops:
  7.2 25.5 %copy-start.24 = (s32[1,128]{1,0:T(1,128)S(1)}, s32[1,128]{1,0:T(1,128)}, u32[]{:S(2)}) copy-start(s32[1,128]{1,0:T(1,128)} %param.10) | copy-start | bytes 1540
  7.2 32.9 %copy-start.25 = (f32[1,28]{1,0:T(1,128)S(1)}, f32[1,28]{1,0:T(1,128)}, u32[]{:S(2)}) copy-start(f32[1,28]{1,0:T(1,128)} %param.14) | copy-start | bytes 340
  7.2 74.1 %reduce-scatter.3.cloned.1.call-start = ((), (), s32[]{:S(2)}) async-start(), calls=%async_computation.2 | async-start | bytes 98304 | tf_op jit(solution)/shard_map/reduce_scatter | solution.py:124
  7.3 10.3 %collective-permute-start = (bf16[32,1792]{1,0:T(8,128)(2,1)}, bf16[32,1792]{1,0:T(8,128)(2,1)S(1)}, u32[]{:S(2)}, u32[]{:S(2)}) collective-permute-start(bf16[32,1792]{1,0:T(8,128)(2,1)} %bitcast.230), channel_id=1, source_target_pairs={{0,2},{2,4},{4,6},{6,8},{8,10},{10,12},{12,14},{14,0},{1,3},{3,5},... | collective-permute-start | bytes 344072 | tf_op jit(solution)/shard_map/ppermute | solution.py:119
  11.5 21.1 %collective-permute-start.8 = (s32[1]{0:T(128)}, s32[1]{0:T(128)}, u32[]{:S(2)}, u32[]{:S(2)}) collective-permute-start(s32[1]{0:T(128)} %bitcast.19), channel_id=1, source_target_pairs={{0,2},{2,4},{4,6},{6,8},{8,10},{10,12},{12,14},{1,3},{3,5},{5,7},{... | collective-permute-start | bytes 20 | tf_op jit(solution)/shard_map/ppermute | solution.py:12
  17.6 7.5 %collective-permute-start.1 = (bf16[32,1792]{1,0:T(8,128)(2,1)S(1)}, bf16[32,1792]{1,0:T(8,128)(2,1)S(1)}, u32[]{:S(2)}, u32[]{:S(2)}) collective-permute-start(bf16[32,1792]{1,0:T(8,128)(2,1)S(1)} %collective-permute-done), channel_id=1, source_target_pairs={{0,2},{2,4},{4,6},{6,8},{8,10},{10,12},{12,14},{14,0},{1,3},{3,5},... | collective-permute-start | bytes 344072 | tf_op jit(solution)/shard_map/ppermute | solution.py:119
  18.6 49.7 %copy-start.5 = (bf16[1,32,1792]{2,1,0:T(8,128)(2,1)S(1)}, bf16[1,32,1792]{2,1,0:T(8,128)(2,1)}, u32[]{:S(2)}) copy-start(bf16[1,32,1792]{2,1,0:T(8,128)(2,1)} %param.12) | copy-start | bytes 344068
  19.2 38.6 %copy-start.2 = (f32[28,1,128]{0,2,1:T(8,128)}, f32[28,1,128]{0,2,1:T(8,128)S(1)}, u32[]{:S(2)}) copy-start(f32[28,1,128]{0,2,1:T(8,128)S(1)} %copy.83) | copy-start | bytes 43012
  25.1 7.5 %collective-permute-start.2 = (bf16[32,1792]{1,0:T(8,128)(2,1)S(1)}, bf16[32,1792]{1,0:T(8,128)(2,1)S(1)}, u32[]{:S(2)}, u32[]{:S(2)}) collective-permute-start(bf16[32,1792]{1,0:T(8,128)(2,1)S(1)} %collective-permute-done.1), channel_id=1, source_target_pairs={{0,2},{2,4},{4,6},{6,8},{8,10},{10,12},{12,14},{14,0},{1,3},{3,5},... | collective-permute-start | bytes 344072 | tf_op jit(solution)/shard_map/ppermute | solution.py:119
  25.1 31.1 %copy-start.39 = (f32[28]{0:T(128)}, f32[28]{0:T(128)S(1)}, u32[]{:S(2)}) copy-start(f32[28]{0:T(128)S(1)} %negate_bitcast_fusion) | copy-start | bytes 340
  32.6 7.5 %collective-permute-start.3 = (bf16[32,1792]{1,0:T(8,128)(2,1)S(1)}, bf16[32,1792]{1,0:T(8,128)(2,1)S(1)}, u32[]{:S(2)}, u32[]{:S(2)}) collective-permute-start(bf16[32,1792]{1,0:T(8,128)(2,1)S(1)} %collective-permute-done.2), channel_id=1, source_target_pairs={{0,2},{2,4},{4,6},{6,8},{8,10},{10,12},{12,14},{14,0},{1,3},{3,5},... | collective-permute-start | bytes 344072 | tf_op jit(solution)/shard_map/ppermute | solution.py:119
  34.0 22.3 %copy-start.36 = (f32[128]{0:T(128)}, f32[128]{0:T(128)S(1)}, u32[]{:S(2)}) copy-start(f32[128]{0:T(128)S(1)} %get-tuple-element.44) | copy-start | bytes 1540
  34.0 38.9 %copy-start.20 = (pred[128]{0:T(512)(128)(4,1)}, pred[128]{0:T(512)(128)(4,1)S(1)}, u32[]{:S(2)}) copy-start(pred[128]{0:T(512)(128)(4,1)S(1)} %get-tuple-element.31) | copy-start | bytes 388
  34.0 38.9 %copy-start.22 = (f32[128]{0:T(128)}, f32[128]{0:T(128)S(1)}, u32[]{:S(2)}) copy-start(f32[128]{0:T(128)S(1)} %get-tuple-element.32) | copy-start | bytes 1540
  40.1 7.5 %collective-permute-start.4 = (bf16[32,1792]{1,0:T(8,128)(2,1)S(1)}, bf16[32,1792]{1,0:T(8,128)(2,1)S(1)}, u32[]{:S(2)}, u32[]{:S(2)}) collective-permute-start(bf16[32,1792]{1,0:T(8,128)(2,1)S(1)} %collective-permute-done.3), channel_id=1, source_target_pairs={{0,2},{2,4},{4,6},{6,8},{8,10},{10,12},{12,14},{14,0},{1,3},{3,5},... | collective-permute-start | bytes 344072 | tf_op jit(solution)/shard_map/ppermute | solution.py:119
  40.4 33.1 %copy-start.15 = (f32[128,28]{0,1:T(8,128)}, f32[128,28]{0,1:T(8,128)S(1)}, u32[]{:S(2)}) copy-start(f32[128,28]{0,1:T(8,128)S(1)} %get-tuple-element.48) | copy-start | bytes 43012
  47.6 8.6 %collective-permute-start.5 = (bf16[32,1792]{1,0:T(8,128)(2,1)S(1)}, bf16[32,1792]{1,0:T(8,128)(2,1)S(1)}, u32[]{:S(2)}, u32[]{:S(2)}) collective-permute-start(bf16[32,1792]{1,0:T(8,128)(2,1)S(1)} %collective-permute-done.4), channel_id=1, source_target_pairs={{0,2},{2,4},{4,6},{6,8},{8,10},{10,12},{12,14},{14,0},{1,3},{3,5},... | collective-permute-start | bytes 344072 | tf_op jit(solution)/shard_map/ppermute | solution.py:119
  47.6 25.9 %copy-start.27 = (f32[28]{0:T(128)}, f32[28]{0:T(128)S(1)}, u32[]{:S(2)}) copy-start(f32[28]{0:T(128)S(1)} %slice_bitcast_fusion) | copy-start | bytes 340
  56.2 7.5 %collective-permute-start.6 = (bf16[32,1792]{1,0:T(8,128)(2,1)S(1)}, bf16[32,1792]{1,0:T(8,128)(2,1)S(1)}, u32[]{:S(2)}, u32[]{:S(2)}) collective-permute-start(bf16[32,1792]{1,0:T(8,128)(2,1)S(1)} %collective-permute-done.5), channel_id=1, source_target_pairs={{0,2},{2,4},{4,6},{6,8},{8,10},{10,12},{12,14},{14,0},{1,3},{3,5},... | collective-permute-start | bytes 344072 | tf_op jit(solution)/shard_map/ppermute | solution.py:119
  76.4 143.1 %reduce-scatter.5.cloned.1.call-start = ((), (), s32[]{:S(2)}) async-start(), calls=%async_computation.3 | async-start | bytes 1032192 | tf_op jit(solution)/shard_map/reduce_scatter | solution.py:185
  83.4 10.0 %collective-permute-start.7 = (bf16[28,4096]{1,0:T(8,128)(2,1)}, bf16[28,4096]{1,0:T(8,128)(2,1)}, u32[]{:S(2)}, u32[]{:S(2)}) collective-permute-start(bf16[28,4096]{1,0:T(8,128)(2,1)} %convert_element_type.193), channel_id=1, source_target_pairs={{0,2},{2,4},{4,6},{6,8},{8,10},{10,12},{12,14},{1,3},{3,5},{5,7},{... | collective-permute-start | bytes 688136 | tf_op jit(solution)/shard_map/ppermute | solution.py:12
  91.1 15.8 %collective-permute-start.13 = (bf16[28,4096]{1,0:T(8,128)(2,1)S(1)}, bf16[28,4096]{1,0:T(8,128)(2,1)S(1)}, u32[]{:S(2)}, u32[]{:S(2)}) collective-permute-start(bf16[28,4096]{1,0:T(8,128)(2,1)S(1)} %convert_element_type.204), channel_id=1, source_target_pairs={{2,0},{4,2},{6,4},{8,6},{10,8},{12,10},{14,12},{3,1},{5,3},{7,5},{... | collective-permute-start | bytes 688136 | tf_op jit(solution)/shard_map/ppermute | solution.py:12
  94.5 12.5 %collective-permute-start.10 = (bf16[28,4096]{1,0:T(8,128)(2,1)S(1)}, bf16[28,4096]{1,0:T(8,128)(2,1)S(1)}, u32[]{:S(2)}, u32[]{:S(2)}) collective-permute-start(bf16[28,4096]{1,0:T(8,128)(2,1)S(1)} %fusion.57), channel_id=1, source_target_pairs={{0,4},{2,6},{4,8},{6,10},{8,12},{10,14},{1,5},{3,7},{5,9},{7,11},{... | collective-permute-start | bytes 688136 | tf_op jit(solution)/shard_map/ppermute | solution.py:12
  99.8 5.9 %collective-permute-start.14 = (f32[28]{0:T(128)S(1)}, f32[28]{0:T(128)S(1)}, u32[]{:S(2)}, u32[]{:S(2)}) collective-permute-start(f32[28]{0:T(128)S(1)} %exponential_multiply_fusion.1), channel_id=1, source_target_pairs={{2,0},{4,2},{6,4},{8,6},{10,8},{12,10},{14,12},{3,1},{5,3},{7,5},{... | collective-permute-start | bytes 344 | tf_op jit(solution)/shard_map/ppermute | solution.py:12
  101.1 5.8 %collective-permute-start.9 = (f32[28]{0:T(128)S(1)}, f32[28]{0:T(128)S(1)}, u32[]{:S(2)}, u32[]{:S(2)}) collective-permute-start(f32[28]{0:T(128)S(1)} %exponential_multiply_fusion.1), channel_id=1, source_target_pairs={{0,2},{2,4},{4,6},{6,8},{8,10},{10,12},{12,14},{1,3},{3,5},{5,7},{... | collective-permute-start | bytes 344 | tf_op jit(solution)/shard_map/ppermute | solution.py:12
  105.7 27.6 %copy-start.31 = (f32[28]{0:T(128)}, f32[28]{0:T(128)S(1)}, u32[]{:S(2)}) copy-start(f32[28]{0:T(128)S(1)} %collective-permute-done.14) | copy-start | bytes 340
  108.9 9.8 %collective-permute-start.15 = (bf16[28,4096]{1,0:T(8,128)(2,1)S(1)}, bf16[28,4096]{1,0:T(8,128)(2,1)S(1)}, u32[]{:S(2)}, u32[]{:S(2)}) collective-permute-start(bf16[28,4096]{1,0:T(8,128)(2,1)S(1)} %get-tuple-element.41), channel_id=1, source_target_pairs={{4,0},{6,2},{8,4},{10,6},{12,8},{14,10},{5,1},{7,3},{9,5},{11,7},{... | collective-permute-start | bytes 688136 | tf_op jit(solution)/shard_map/ppermute | solution.py:12
  110.9 23.2 %collective-permute-start.12 = (bf16[28,4096]{1,0:T(8,128)(2,1)}, bf16[28,4096]{1,0:T(8,128)(2,1)}, u32[]{:S(2)}, u32[]{:S(2)}) collective-permute-start(bf16[28,4096]{1,0:T(8,128)(2,1)} %get-tuple-element.40), channel_id=1, source_target_pairs={{0,8},{2,10},{4,12},{6,14},{1,9},{3,11},{5,13},{7,15},{16,24},{18,... | collective-permute-start | bytes 688136 | tf_op jit(solution)/shard_map/ppermute | solution.py:12
  119.6 14.5 %collective-permute-start.17 = (bf16[28,4096]{1,0:T(8,128)(2,1)}, bf16[28,4096]{1,0:T(8,128)(2,1)}, u32[]{:S(2)}, u32[]{:S(2)}) collective-permute-start(bf16[28,4096]{1,0:T(8,128)(2,1)} %fusion.46), channel_id=1, source_target_pairs={{8,0},{10,2},{12,4},{14,6},{9,1},{11,3},{13,5},{15,7},{24,16},{26,... | collective-permute-start | bytes 688136 | tf_op jit(solution)/shard_map/ppermute | solution.py:12
  122.5 5.4 %collective-permute-start.11 = (f32[28]{0:T(128)S(1)}, f32[28]{0:T(128)S(1)}, u32[]{:S(2)}, u32[]{:S(2)}) collective-permute-start(f32[28]{0:T(128)S(1)} %get-tuple-element.42), channel_id=1, source_target_pairs={{0,4},{2,6},{4,8},{6,10},{8,12},{10,14},{1,5},{3,7},{5,9},{7,11},{... | collective-permute-start | bytes 344 | tf_op jit(solution)/shard_map/ppermute | solution.py:12
  126.6 6.7 %collective-permute-start.16 = (f32[28]{0:T(128)S(1)}, f32[28]{0:T(128)S(1)}, u32[]{:S(2)}, u32[]{:S(2)}) collective-permute-start(f32[28]{0:T(128)S(1)} %get-tuple-element.43), channel_id=1, source_target_pairs={{4,0},{6,2},{8,4},{10,6},{12,8},{14,10},{5,1},{7,3},{9,5},{11,7},{... | collective-permute-start | bytes 344 | tf_op jit(solution)/shard_map/ppermute | solution.py:12
  161.3 23.9 %collective-permute-start.18 = (bf16[1,128,1792]{2,1,0:T(8,128)(2,1)S(1)}, bf16[1,128,1792]{2,1,0:T(8,128)(2,1)S(1)}, u32[]{:S(2)}, u32[]{:S(2)}) collective-permute-start(bf16[1,128,1792]{2,1,0:T(8,128)(2,1)S(1)} %fusion.1), channel_id=1, source_target_pairs={{16,0},{17,1},{18,2},{19,3},{20,4},{21,5},{22,6},{23,7},{24,8},{25... | collective-permute-start | bytes 1376264 | tf_op jit(solution)/shard_map/ppermute | solution.py:12
  (33 other events, 198.8 us)
Sparse Core Ops, SparseCore 0:
  76.5 4.6 reduce-scatter.2
  157.0 62.4 reduce-scatter.4
